TPU v7x, 256 devices: a whole 4x4x8 slice. The times are simulated.
256 devices in a mesh: dom: 32 (over y_hi, z, core), tp: 8 (over x, y_lo).
Axes of the slice: x: 4, y: 4 (y_hi: 2, y_lo: 2; y = y_hi * 2 + y_lo), z: 8, core: 2. Of those that a mesh axis runs over, the one named last changes fastest.
Arguments:
- hidden_in: bfloat16 [448, 64, 4096], P('dom', None, 'tp'), may hold values from -6 to 6
- query_weight: bfloat16 [4096, 4096], P('dom', 'tp'), may hold values from -0.09375 to 0.09375
- segment_keys: bfloat16 [448, 64, 1024], P('dom', None, 'tp'), may hold values from -6 to 6
- segment_values: bfloat16 [448, 64, 1024], P('dom', None, 'tp'), may hold values from -6 to 6
- prefix_keys: bfloat16 [32, 256, 1024], P('dom', None, 'tp'), may hold values from -80 to 80
- prefix_values: bfloat16 [32, 256, 1024], P('dom', None, 'tp'), may hold values from -6 to 6
- ancestors: int32 [448], P('dom'), may hold values from 0 to 31, as said below
- twist_weights: float32 [448], P('dom'), may hold values from 0.25 to 4
- out_grad: bfloat16 [448, 64, 4096], P('dom', None, 'tp'), may hold values from -24 to 24
Outputs:
- grad_query_weight: bfloat16 [4096, 4096], P('dom', 'tp')
- grad_segment_keys: bfloat16 [448, 64, 1024], P('dom', None, 'tp')
- grad_segment_values: bfloat16 [448, 64, 1024], P('dom', None, 'tp')
- grad_prefix_keys: float32 [32, 256, 1024], P('dom', None, 'tp')
- grad_prefix_values: float32 [32, 256, 1024], P('dom', None, 'tp')
Inputs may be any that keep to these rules, and one draw needn't show every extreme that they name: `ancestors`: among the 14 consecutive particles of one device, no ancestor is named more than 2 times, and one ancestor, the same for all devices, is named exactly 2 times on every device.
All inputs are finite; a program needn't handle non-finite values.
Results may differ from a plain program's by a relative error of at most 0.02.
The roundings to bfloat16 on the way count: a program that leaves them out, or rounds other values in their place, can miss the bound.
Values may be sent and summed in bfloat16 or wider, within the bound.
No kernel may reach another device: no remote copies, remote signals or barrier semaphores. Data moves between devices by JAX's collectives and lax.ppermute only.
A program may use at most 128 MiB of HBM per device.

v0:
```python
import math
import jax
import jax.numpy as jnp
from jax import lax
from jax.sharding import PartitionSpec as P

HD = 128


def attend(queries, scaled, seg_keys, seg_values, pre_keys, pre_values):
    factor = 1.0 / math.sqrt(queries.shape[-1])
    score_pre = (
        jnp.einsum("bikgd,bjkd->bkgij", queries, pre_keys, preferred_element_type=jnp.float32)
        * factor
    )
    score_seg = (
        jnp.einsum("bikgd,bjkd->bkgij", queries, seg_keys, preferred_element_type=jnp.float32)
        * factor
    )
    length = queries.shape[1]
    causal = lax.broadcasted_iota(jnp.int32, (length, length), 0) >= lax.broadcasted_iota(
        jnp.int32, (length, length), 1
    )
    score_seg = jnp.where(causal, score_seg, -jnp.inf)
    row_max = jnp.maximum(jnp.max(score_pre, -1), jnp.max(score_seg, -1))[..., None]
    exp_pre = jnp.exp(score_pre - row_max)
    exp_seg = jnp.exp(score_seg - row_max)
    denominator = (jnp.sum(exp_pre, -1) + jnp.sum(exp_seg, -1))[..., None]
    prob_pre = exp_pre / denominator
    prob_seg = exp_seg / denominator
    dprob_pre = jnp.einsum(
        "bikgd,bjkd->bkgij", scaled, pre_values, preferred_element_type=jnp.float32
    )
    dprob_seg = jnp.einsum(
        "bikgd,bjkd->bkgij", scaled, seg_values, preferred_element_type=jnp.float32
    )
    row_delta = (jnp.sum(prob_pre * dprob_pre, -1) + jnp.sum(prob_seg * dprob_seg, -1))[..., None]
    dscore_pre = (prob_pre * (dprob_pre - row_delta)).astype(jnp.bfloat16)
    dscore_seg = (prob_seg * (dprob_seg - row_delta)).astype(jnp.bfloat16)
    grad_q = (
        jnp.einsum("bkgij,bjkd->bikgd", dscore_pre, pre_keys, preferred_element_type=jnp.float32)
        + jnp.einsum("bkgij,bjkd->bikgd", dscore_seg, seg_keys, preferred_element_type=jnp.float32)
    ) * factor
    grad_pk = (
        jnp.einsum("bkgij,bikgd->bjkd", dscore_pre, queries, preferred_element_type=jnp.float32)
        * factor
    )
    grad_pv = jnp.einsum(
        "bkgij,bikgd->bjkd",
        prob_pre.astype(jnp.bfloat16),
        scaled,
        preferred_element_type=jnp.float32,
    )
    grad_sk = (
        jnp.einsum("bkgij,bikgd->bjkd", dscore_seg, queries, preferred_element_type=jnp.float32)
        * factor
    )
    grad_sv = jnp.einsum(
        "bkgij,bikgd->bjkd",
        prob_seg.astype(jnp.bfloat16),
        scaled,
        preferred_element_type=jnp.float32,
    )
    return (
        grad_q.astype(jnp.bfloat16),
        grad_sk.astype(jnp.bfloat16),
        grad_sv.astype(jnp.bfloat16),
        grad_pk,
        grad_pv,
    )


def local(
    hidden_in,
    query_weight,
    segment_keys,
    segment_values,
    prefix_keys,
    prefix_values,
    ancestors,
    twist_weights,
    out_grad,
):
    particles_here = hidden_in.shape[0]
    length = hidden_in.shape[1]
    features = lax.all_gather(hidden_in, "tp", axis=2, tiled=True)
    token_rows = features.reshape(particles_here * length, features.shape[2])
    width_q = query_weight.shape[1]
    width_kv = segment_keys.shape[2]
    kv_heads = width_kv // HD
    group_size = width_q // width_kv
    prefix = prefix_keys.shape[1]
    columns = token_rows
    queries = jnp.dot(
        columns,
        lax.all_gather(query_weight, "dom", axis=0, tiled=True),
        preferred_element_type=jnp.float32,
    ).astype(jnp.bfloat16)
    queries = queries.reshape(particles_here, length, width_q)
    scaled = (out_grad.astype(jnp.float32) * twist_weights[:, None, None]).astype(jnp.bfloat16)
    owners = lax.axis_size("dom")
    capacity = max(2, (2 * particles_here + owners - 1) // owners)
    positions = jnp.arange(particles_here, dtype=jnp.int32)
    shared = ancestors[:, None] == ancestors[None, :]
    slot_rank = jnp.sum(
        (shared & (positions[:, None] > positions[None, :])).astype(jnp.int32), axis=1
    )
    owner_ids = jnp.arange(owners, dtype=jnp.int32)
    slot_ids = jnp.arange(capacity, dtype=jnp.int32)
    slot_table = (
        (ancestors[None, None, :] == owner_ids[:, None, None])
        & (slot_rank[None, None, :] == slot_ids[None, :, None])
    ).astype(jnp.bfloat16)

    def to_slots(block):
        return jnp.einsum(
            "acp,piw->aciw", slot_table, block, preferred_element_type=jnp.float32
        ).astype(jnp.bfloat16)

    def from_slots(block):
        return jnp.einsum(
            "acp,aciw->piw", slot_table, block, preferred_element_type=jnp.float32
        ).astype(jnp.bfloat16)

    arrived = (
        lax.all_to_all(to_slots(queries), "dom", split_axis=0, concat_axis=0, tiled=True),
        lax.all_to_all(to_slots(scaled), "dom", split_axis=0, concat_axis=0, tiled=True),
        lax.all_to_all(to_slots(segment_keys), "dom", split_axis=0, concat_axis=0, tiled=True),
        lax.all_to_all(to_slots(segment_values), "dom", split_axis=0, concat_axis=0, tiled=True),
    )
    sources = max(
        (
            divisor
            for divisor in range(1, owners + 1)
            if owners % divisor == 0 and divisor * capacity <= max(particles_here, capacity)
        )
    )
    block_count = owners // sources
    slot_count = sources * capacity
    own_keys = jnp.broadcast_to(
        prefix_keys.reshape(1, prefix, kv_heads, HD), (slot_count, prefix, kv_heads, HD)
    )
    own_values = jnp.broadcast_to(
        prefix_values.reshape(1, prefix, kv_heads, HD), (slot_count, prefix, kv_heads, HD)
    )

    def handle(carried, entry):
        slot_q, slot_o, slot_k, slot_v = entry
        grad_q, grad_sk, grad_sv, grad_pk, grad_pv = attend(
            slot_q.reshape(slot_count, length, kv_heads, group_size, HD),
            slot_o.reshape(slot_count, length, kv_heads, group_size, HD),
            slot_k.reshape(slot_count, length, kv_heads, HD),
            slot_v.reshape(slot_count, length, kv_heads, HD),
            own_keys,
            own_values,
        )
        updated = (carried[0] + jnp.sum(grad_pk, 0), carried[1] + jnp.sum(grad_pv, 0))
        return (
            updated,
            (
                grad_q.reshape(slot_count, length, width_q),
                grad_sk.reshape(slot_count, length, width_kv),
                grad_sv.reshape(slot_count, length, width_kv),
            ),
        )

    blocks = tuple(
        (member.reshape(block_count, slot_count, length, member.shape[-1]) for member in arrived)
    )
    nothing = jnp.zeros((prefix, kv_heads, HD), jnp.float32)
    (sum_keys, sum_values), (out_q, out_k, out_v) = lax.scan(handle, (nothing, nothing), blocks)
    returned = (
        lax.all_to_all(
            out_q.reshape(owners, capacity, length, width_q),
            "dom",
            split_axis=0,
            concat_axis=0,
            tiled=True,
        ),
        lax.all_to_all(
            out_k.reshape(owners, capacity, length, width_kv),
            "dom",
            split_axis=0,
            concat_axis=0,
            tiled=True,
        ),
        lax.all_to_all(
            out_v.reshape(owners, capacity, length, width_kv),
            "dom",
            split_axis=0,
            concat_axis=0,
            tiled=True,
        ),
    )
    grad_queries = from_slots(returned[0])
    grad_seg_keys = from_slots(returned[1])
    grad_seg_values = from_slots(returned[2])
    grad_pre_keys = sum_keys.reshape(1, prefix, width_kv)
    grad_pre_values = sum_values.reshape(1, prefix, width_kv)
    grad_rows = grad_queries.reshape(particles_here * length, width_q)
    columns = token_rows
    grad_weight = lax.psum_scatter(
        jnp.einsum("tc,tq->cq", columns, grad_rows, preferred_element_type=jnp.float32).astype(
            jnp.bfloat16
        ),
        "dom",
        scatter_dimension=0,
        tiled=True,
    )
    return (grad_weight, grad_seg_keys, grad_seg_values, grad_pre_keys, grad_pre_values)


def solution(mesh):
    return jax.shard_map(
        local,
        mesh=mesh,
        in_specs=(
            P("dom", None, "tp"),
            P("dom", "tp"),
            P("dom", None, "tp"),
            P("dom", None, "tp"),
            P("dom", None, "tp"),
            P("dom", None, "tp"),
            P("dom"),
            P("dom"),
            P("dom", None, "tp"),
        ),
        out_specs=(
            P("dom", "tp"),
            P("dom", None, "tp"),
            P("dom", None, "tp"),
            P("dom", None, "tp"),
            P("dom", None, "tp"),
        ),
        check_vma=False,
    )
```

profile of v0, /device:TPU:2, one launch (start us, length us, event | category | flops | bytes accessed | tf_op | source)
XLA Modules:
  0.0 876.4 jit_solution(134274365021562520)
XLA Ops:
  13.3 11.6 %all-to-all-start.3 = ((bf16[32,2,64,128]{3,2,1,0:T(8,128)(2,1)}), bf16[32,2,64,128]{3,2,1,0:T(8,128)(2,1)S(1)}, u32[]{:S(2)}, u32[]{:S(2)}) async-start(bf16[32,2,64,128]{3,2,1,0:T(8,128)(2,1)} %copy.158), calls=%async_computation.3 | async-start | bytes 2097152 | tf_op jit(solution)/shard_map/all_to_all | solution.py:129
  26.9 32.4 %all-to-all-done.3 = bf16[32,2,64,128]{3,2,1,0:T(8,128)(2,1)S(1)} async-done(((bf16[32,2,64,128]{3,2,1,0:T(8,128)(2,1)}), bf16[32,2,64,128]{3,2,1,0:T(8,128)(2,1)S(1)}, u32[]{:S(2)}, u32[]{:S(2)}) %all-to-all-start.3) | async-done | bytes 1048608 | tf_op jit(solution)/shard_map/all_to_all | solution.py:129
  59.3 4.7 all-to-all-start.1
  65.6 4.4 copy.156
  70.0 27.1 %all-to-all-done.1 = bf16[32,2,64,128]{3,2,1,0:T(8,128)(2,1)} async-done(((bf16[32,2,64,128]{3,2,1,0:T(8,128)(2,1)}), bf16[32,2,64,128]{3,2,1,0:T(8,128)(2,1)}, u32[]{:S(2)}, u32[]{:S(2)}) %all-to-all-start.1) | async-done | bytes 1048608 | tf_op jit(solution)/shard_map/all_to_all | solution.py:128
  97.1 5.4 all-to-all-start.2
  102.6 21.5 %all-gather.5.cloned.1.call-done = bf16[4096,512]{1,0:T(8,128)(2,1)} async-done(((bf16[128,512]{1,0:T(8,128)(2,1)}), bf16[4096,512]{1,0:T(8,128)(2,1)}) %all-gather.5.cloned.1.call-update) | async-done | bytes 4194320 | tf_op jit(solution)/shard_map/all_gather | solution.py:96
  124.0 178.3 %all-gather.3.cloned.1.call-done = bf16[14,64,4096]{2,1,0:T(8,128)(2,1)} async-done(((bf16[14,64,512]{2,1,0:T(8,128)(2,1)}), bf16[14,64,4096]{2,1,0:T(8,128)(2,1)}) %all-gather.3.cloned.1.call-update) | async-done | bytes 7340048 | tf_op jit(solution)/shard_map/all_gather | solution.py:86
  302.3 8.2 convolution_convert_fusion.4
  311.9 4.4 copy.152
  316.3 8.2 all-to-all-start
  324.8 96.4 %all-to-all-done = bf16[32,2,64,512]{3,2,1,0:T(8,128)(2,1)} async-done(((bf16[32,2,64,512]{3,2,1,0:T(8,128)(2,1)}), bf16[32,2,64,512]{3,2,1,0:T(8,128)(2,1)}, u32[]{:S(2)}, u32[]{:S(2)}) %all-to-all-start) | async-done | bytes 4194336 | tf_op jit(solution)/shard_map/all_to_all | solution.py:126
  421.2 185.9 %while.19 = (s32[]{:T(128)}, f32[256,1,128]{0,2,1:T(8,128)S(1)}, f32[256,1,128]{0,2,1:T(8,128)S(1)}, bf16[8,8,64,512]{3,2,1,0:T(8,128)(2,1)}, bf16[8,8,64,128]{3...) while((s32[]{:T(128)}, f32[256,1,128]{0,2,1:T(8,128)S(1)}, ...), condition=%wide.region_9.10_spmd.clone, body=%wide.region_1.9_spmd.clone.sunk | while | flops 851605504 | bytes 65064360 | solution.py:171
  422.2 2.1 constant_dynamic-slice_fusion.3
  428.8 2.0 reshape.285
  439.2 2.1 fusion.133
  445.5 2.1 constant_dynamic-slice_fusion.3
  452.0 2.0 reshape.285
  462.5 2.1 fusion.133
  468.7 2.1 constant_dynamic-slice_fusion.3
  475.3 2.0 reshape.285
  485.7 2.1 fusion.133
  491.9 2.1 constant_dynamic-slice_fusion.3
  498.5 2.0 reshape.285
  508.9 2.1 fusion.133
  515.2 2.1 constant_dynamic-slice_fusion.3
  521.7 2.0 reshape.285
  532.2 2.1 fusion.133
  538.4 2.1 constant_dynamic-slice_fusion.3
  544.9 2.0 reshape.285
  555.4 2.1 fusion.133
  561.6 2.1 constant_dynamic-slice_fusion.3
  568.2 2.0 reshape.285
  578.6 2.1 fusion.133
  584.9 2.1 constant_dynamic-slice_fusion.3
  601.8 2.1 fusion.133
  607.1 6.5 copy.159
  613.6 103.7 %all_to_all.35 = bf16[32,2,64,512]{3,1,2,0:T(2,128)(2,1)S(1)} all-to-all(bf16[32,2,64,512]{3,1,2,0:T(2,128)(2,1)S(1)} %copy.159), channel_id=1, replica_groups=mesh['dom'=32,'tp'=8] {'dom'}, dimensions={0} | all-to-all | bytes 8388608 | tf_op jit(solution)/shard_map/all_to_all | solution.py:173
  717.4 2.4 bitcast_convert_fusion.1
  719.8 9.5 %fusion.58 = bf16[4096,512]{0,1:T(8,128)(2,1)} fusion(bf16[14,64,4096]{2,1,0:T(8,128)(2,1)} %all-gather.3.cloned.1.call-done, bf16[14,64,512]{2,0,1:T(8,128)(2,1)S(1)} %bitcast_convert_fusion.1), kind=kOutput, calls=%fused_computation.77 | convolution fusion | flops 3760193536 | bytes 12451840 | tf_op jit(solution)/shard_map/tc,tq->cq/dot_general | solution.py:203
  729.3 6.5 copy.184
  736.9 2.1 copy.162
  739.0 3.9 all-to-all-start.5
  742.9 2.1 copy.164
  745.0 27.9 %all-to-all-done.5 = bf16[32,2,64,128]{3,1,2,0:T(2,128)(2,1)S(1)} async-done(((bf16[32,2,64,128]{3,1,2,0:T(2,128)(2,1)}), bf16[32,2,64,128]{3,1,2,0:T(2,128)(2,1)S(1)}, u32[]{:S(2)}, u32[]{:S(2)}) %all-to-all-start.5) | async-done | bytes 1048608 | tf_op jit(solution)/shard_map/all_to_all | solution.py:180
  772.9 4.0 all-to-all-start.6
  779.8 29.1 %all-to-all-done.6 = bf16[32,2,64,128]{3,1,2,0:T(2,128)(2,1)S(1)} async-done(((bf16[32,2,64,128]{3,1,2,0:T(2,128)(2,1)}), bf16[32,2,64,128]{3,1,2,0:T(2,128)(2,1)S(1)}, u32[]{:S(2)}, u32[]{:S(2)}) %all-to-all-start.6) | async-done | bytes 1048608 | tf_op jit(solution)/shard_map/all_to_all | solution.py:187
  810.4 59.2 %reduce-scatter.4.cloned.1.call-done = bf16[128,512]{1,0:T(8,128)(2,1)} async-done(((bf16[4096,512]{1,0:T(8,128)(2,1)}), bf16[128,512]{1,0:T(8,128)(2,1)}) %reduce-scatter.4.cloned.1.call-update) | async-done | bytes 131088
  (377 shorter events, 154.2 us)
Async XLA Ops:
  7.2 17.7 %copy-start.13 = (bf16[14,64,128]{2,1,0:T(8,128)(2,1)S(1)}, bf16[14,64,128]{2,1,0:T(8,128)(2,1)}, u32[]{:S(2)}) copy-start(bf16[14,64,128]{2,1,0:T(8,128)(2,1)} %param.13) | copy-start | bytes 688132
  7.2 116.9 %all-gather.5.cloned.1.call-start = ((), (), s32[]{:S(2)}) async-start(), calls=%async_computation.9 | async-start | bytes 4325376 | tf_op jit(solution)/shard_map/all_gather | solution.py:96
  7.9 294.4 %all-gather.3.cloned.1.call-start = ((), (), s32[]{:S(2)}) async-start(), calls=%async_computation.8 | async-start | bytes 8257536 | tf_op jit(solution)/shard_map/all_gather | solution.py:86
  13.3 50.7 %copy-start.12 = (bf16[14,64,512]{2,1,0:T(8,128)(2,1)S(1)}, bf16[14,64,512]{2,1,0:T(8,128)(2,1)}, u32[]{:S(2)}) copy-start(bf16[14,64,512]{2,1,0:T(8,128)(2,1)} %param.19) | copy-start | bytes 2752516
  13.3 50.7 %copy-start.14 = (f32[14]{0:T(128)S(1)}, f32[14]{0:T(128)}, u32[]{:S(2)}) copy-start(f32[14]{0:T(128)} %param.18) | copy-start | bytes 172
  13.3 46.0 %all-to-all-start.3 = ((bf16[32,2,64,128]{3,2,1,0:T(8,128)(2,1)}), bf16[32,2,64,128]{3,2,1,0:T(8,128)(2,1)S(1)}, u32[]{:S(2)}, u32[]{:S(2)}) async-start(bf16[32,2,64,128]{3,2,1,0:T(8,128)(2,1)} %copy.158), calls=%async_computation.3 | async-start | bytes 2097152 | tf_op jit(solution)/shard_map/all_to_all | solution.py:129
  59.3 37.8 %all-to-all-start.1 = ((bf16[32,2,64,128]{3,2,1,0:T(8,128)(2,1)}), bf16[32,2,64,128]{3,2,1,0:T(8,128)(2,1)}, u32[]{:S(2)}, u32[]{:S(2)}) async-start(bf16[32,2,64,128]{3,2,1,0:T(8,128)(2,1)} %copy.154), calls=%async_computation.1 | async-start | bytes 2097152 | tf_op jit(solution)/shard_map/all_to_all | solution.py:128
  97.1 219.2 %all-to-all-start.2 = ((bf16[32,2,64,512]{3,2,1,0:T(8,128)(2,1)}), bf16[32,2,64,512]{3,2,1,0:T(8,128)(2,1)}, u32[]{:S(2)}, u32[]{:S(2)}) async-start(bf16[32,2,64,512]{3,2,1,0:T(8,128)(2,1)} %copy.156), calls=%async_computation.2 | async-start | bytes 8388608 | tf_op jit(solution)/shard_map/all_to_all | solution.py:127
  316.3 104.9 %copy-start.7 = (bf16[1,256,128]{2,1,0:T(8,128)(2,1)S(1)}, bf16[1,256,128]{2,1,0:T(8,128)(2,1)}, u32[]{:S(2)}) copy-start(bf16[1,256,128]{2,1,0:T(8,128)(2,1)} %param.15) | copy-start | bytes 196612
  316.3 104.9 %all-to-all-start = ((bf16[32,2,64,512]{3,2,1,0:T(8,128)(2,1)}), bf16[32,2,64,512]{3,2,1,0:T(8,128)(2,1)}, u32[]{:S(2)}, u32[]{:S(2)}) async-start(bf16[32,2,64,512]{3,2,1,0:T(8,128)(2,1)} %copy.152), calls=%async_computation | async-start | bytes 8388608 | tf_op jit(solution)/shard_map/all_to_all | solution.py:126
  324.5 545.1 %reduce-scatter.4.cloned.1.call-start = ((), (), s32[]{:S(2)}) async-start(), calls=%async_computation.10 | async-start | bytes 4325376
  433.9 2.2 copy-start.4
  435.7 3.5 copy-start.1
  435.7 5.5 copy-start.6
  439.2 4.8 copy-start.3
  457.2 2.2 copy-start.4
  459.0 3.5 copy-start.1
  459.0 5.5 copy-start.6
  462.5 4.8 copy-start.3
  465.6 2.1 copy-start.9
  480.4 2.2 copy-start.4
  482.2 3.4 copy-start.1
  482.2 5.5 copy-start.6
  485.7 4.8 copy-start.3
  488.8 2.1 copy-start.9
  503.6 2.2 copy-start.4
  505.5 3.5 copy-start.1
  505.5 5.5 copy-start.6
  508.9 4.8 copy-start.3
  526.9 2.2 copy-start.4
  528.7 3.5 copy-start.1
  528.7 5.5 copy-start.6
  532.2 4.8 copy-start.3
  550.1 2.2 copy-start.4
  551.9 3.5 copy-start.1
  551.9 5.5 copy-start.6
  555.4 4.8 copy-start.3
  573.3 2.2 copy-start.4
  575.1 3.5 copy-start.1
  575.1 5.5 copy-start.6
  578.6 4.8 copy-start.3
  596.6 2.2 copy-start.4
  598.4 3.4 copy-start.1
  598.4 5.5 copy-start.6
  601.8 4.8 copy-start.3
  735.7 7.2 copy-start.11
  739.0 33.9 %all-to-all-start.5 = ((bf16[32,2,64,128]{3,1,2,0:T(2,128)(2,1)}), bf16[32,2,64,128]{3,1,2,0:T(2,128)(2,1)S(1)}, u32[]{:S(2)}, u32[]{:S(2)}) async-start(bf16[32,2,64,128]{3,1,2,0:T(2,128)(2,1)} %copy.162), calls=%async_computation.5 | async-start | bytes 2097152 | tf_op jit(solution)/shard_map/all_to_all | solution.py:180
  772.9 36.1 %all-to-all-start.6 = ((bf16[32,2,64,128]{3,1,2,0:T(2,128)(2,1)}), bf16[32,2,64,128]{3,1,2,0:T(2,128)(2,1)S(1)}, u32[]{:S(2)}, u32[]{:S(2)}) async-start(bf16[32,2,64,128]{3,1,2,0:T(2,128)(2,1)} %copy.164), calls=%async_computation.6 | async-start | bytes 2097152 | tf_op jit(solution)/shard_map/all_to_all | solution.py:187
  (47 other events, 80.8 us)
Sparse Core Ops, SparseCore 0:
  10.8 113.2 all-gather.4
  125.8 176.4 all-gather.2
  735.9 133.7 reduce-scatter.3
where the time goes:
time: 885 us; the launch traced here: 876 us
  waiting for transfers between devices  473 us (53%)
  matrix products  131 us (15%)
  blocking collectives  104 us (12%)
  local copies, waits for them, and re-layouts  86.7 us (10%)
  starting transfers between devices  38.1 us (4%)
  other arithmetic  27.5 us (3%)
  between operations  14.2 us (2%)
    all_gather x1, waiting for transfers between devices, local(): features = lax.all_gather(hidden_in, 'tp', axis=2, tiled=True)  178 us
    all_to_all x1, blocking collectives, local(): lax.all_to_all(out_q.reshape(owners, capacity, length, width_q), 'dom', s...  104 us
    all_to_all x1, waiting for transfers between devices, local(): lax.all_to_all(to_slots(queries), 'dom', split_axis=0, concat_axis=0, til...  96.4 us
    unnamed x4, waiting for transfers between devices  60.6 us
    all_to_all x1, waiting for transfers between devices, local(): lax.all_to_all(to_slots(segment_values), 'dom', split_axis=0, concat_axis...  32.4 us
    all_to_all x1, waiting for transfers between devices, local(): lax.all_to_all(out_v.reshape(owners, capacity, length, width_kv), 'dom',...  29.1 us
    all_to_all x1, waiting for transfers between devices, local(): lax.all_to_all(out_k.reshape(owners, capacity, length, width_kv), 'dom',...  27.9 us
    all_to_all x1, waiting for transfers between devices, local(): lax.all_to_all(to_slots(segment_keys), 'dom', split_axis=0, concat_axis=0...  27.1 us
  transfers between devices with their start and end apart: 9, of which 8 were waited for; matrix products, arithmetic and copies ran while one was open for 4% of the time, Pallas kernels for 0%

commit v1 on v0

--- a/solution.py
+++ b/solution.py
@@ -3,6 +3,7 @@
 import jax.numpy as jnp
 from jax import lax
 from jax.sharding import PartitionSpec as P
+from jax.lax import all_to_all, psum
 
 HD = 128
 
@@ -83,7 +84,13 @@
 ):
     particles_here = hidden_in.shape[0]
     length = hidden_in.shape[1]
-    features = lax.all_gather(hidden_in, "tp", axis=2, tiled=True)
+
+    def number_the_tables(base_x):
+        return jnp.concatenate(
+            all_to_all(jnp.stack(psum(1, "tp") * [base_x], axis=0), "tp", 0, 0), axis=2
+        )
+
+    features = number_the_tables(hidden_in)
     token_rows = features.reshape(particles_here * length, features.shape[2])
     width_q = query_weight.shape[1]
     width_kv = segment_keys.shape[2]

time: 885 us -> 855 us (0.966)
  waiting for transfers between devices: 473 us -> 397 us
  blocking collectives: 104 us -> 138 us
  local copies, waits for them, and re-layouts: 86.7 us -> 98.1 us
    all_gather x1 -> x0, waiting for transfers between devices: 178 us -> none  [local(): features = lax.all_gather(hidden_in, 'tp', axis=2, tiled=True)]
    all_to_all x1, waiting for transfers between devices: 0.01 us -> 65.2 us  [local(): lax.all_to_all(to_slots(scaled), 'dom', split_axis=0, concat_axis=0, tile...]
    all_to_all x1, waiting for transfers between devices: 27.1 us -> 89.7 us  [number_the_tables(): all_to_all(jnp.stack(psum(1, 'tp') * [base_x], axis=0), 'tp', 0, 0)]
    all_to_all x0 -> x1, blocking collectives: none -> 33.8 us  [local(): lax.all_to_all(to_slots(segment_keys), 'dom', split_axis=0, concat_axis=0...]
    all_gather x1, waiting for transfers between devices: 21.5 us -> 1.8 us  [local(): lax.all_gather(query_weight, 'dom', axis=0, tiled=True)]
    another operation x16 -> x17, local copies, waits for them, and re-layouts: 16.7 us -> 20.9 us
    unnamed x4 -> x3, waiting for transfers between devices: 60.6 us -> 58.1 us
  transfers between devices with their start and end apart: 9 -> 8, of which waited for: 8 -> 8; matrix products, arithmetic and copies ran while one was open for 4% -> 5% of each run, Pallas kernels for 0% -> 0%
where the time goes in v1:
time: 855 us; the launch traced here: 846 us
  waiting for transfers between devices  397 us (46%)
  blocking collectives  138 us (16%)
  matrix products  130 us (15%)
  local copies, waits for them, and re-layouts  98.1 us (11%)
  starting transfers between devices  38.9 us (5%)
  other arithmetic  27.4 us (3%)
  between operations  14.4 us (2%)
    all_to_all x1, blocking collectives, local(): lax.all_to_all(out_q.reshape(owners, capacity, length, width_q), 'dom', s...  104 us
    all_to_all x1, waiting for transfers between devices, local(): lax.all_to_all(to_slots(queries), 'dom', split_axis=0, concat_axis=0, til...  96.6 us
    all_to_all x1, waiting for transfers between devices, number_the_tables(): all_to_all(jnp.stack(psum(1, 'tp') * [base_x], axis=0), 'tp', 0, 0)  89.7 us
    all_to_all x1, waiting for transfers between devices, local(): lax.all_to_all(to_slots(scaled), 'dom', split_axis=0, concat_axis=0, tile...  65.2 us
    unnamed x3, waiting for transfers between devices  58.1 us
    all_to_all x1, blocking collectives, local(): lax.all_to_all(to_slots(segment_keys), 'dom', split_axis=0, concat_axis=0...  33.8 us
    all_to_all x1, waiting for transfers between devices, local(): lax.all_to_all(out_v.reshape(owners, capacity, length, width_kv), 'dom',...  29.1 us
    all_to_all x1, waiting for transfers between devices, local(): lax.all_to_all(to_slots(segment_values), 'dom', split_axis=0, concat_axis...  29 us
  transfers between devices with their start and end apart: 8, of which 8 were waited for; matrix products, arithmetic and copies ran while one was open for 5% of the time, Pallas kernels for 0%

profile of v1, /device:TPU:2, one launch (start us, length us, event | category | flops | bytes accessed | tf_op | source)
XLA Modules:
  0.0 845.8 jit_solution(2044981689406239501)
XLA Ops:
  11.8 11.7 %all-to-all-start.4 = ((bf16[32,2,64,128]{3,2,1,0:T(8,128)(2,1)}), bf16[32,2,64,128]{3,2,1,0:T(8,128)(2,1)}, u32[]{:S(2)}, u32[]{:S(2)}) async-start(bf16[32,2,64,128]{3,2,1,0:T(8,128)(2,1)} %copy.103), calls=%async_computation.4 | async-start | bytes 2097152 | tf_op jit(solution)/shard_map/all_to_all | solution.py:136
  24.5 29.0 %all-to-all-done.4 = bf16[32,2,64,128]{3,2,1,0:T(8,128)(2,1)} async-done(((bf16[32,2,64,128]{3,2,1,0:T(8,128)(2,1)}), bf16[32,2,64,128]{3,2,1,0:T(8,128)(2,1)}, u32[]{:S(2)}, u32[]{:S(2)}) %all-to-all-start.4) | async-done | bytes 1048608 | tf_op jit(solution)/shard_map/all_to_all | solution.py:136
  53.5 33.8 %all_to_all.40 = bf16[32,2,64,128]{3,2,1,0:T(8,128)(2,1)} all-to-all(bf16[32,2,64,128]{3,2,1,0:T(8,128)(2,1)S(1)} %copy.99), channel_id=1, replica_groups=mesh['dom'=32,'tp'=8] {'dom'}, dimensions={0} | all-to-all | bytes 2097152 | tf_op jit(solution)/shard_map/all_to_all | solution.py:135
  87.3 3.9 stack.2
  91.2 5.4 all-to-all-start
  99.0 4.4 copy.101
  103.4 89.7 %all-to-all-done = bf16[8,14,64,512]{3,2,1,0:T(8,128)(2,1)} async-done(((bf16[8,14,64,512]{3,2,1,0:T(8,128)(2,1)}), bf16[8,14,64,512]{3,2,1,0:T(8,128)(2,1)}, u32[]{:S(2)}, u32[]{:S(2)}) %all-to-all-start) | async-done | bytes 7340064 | tf_op jit(solution)/shard_map/all_to_all | solution.py:90
  193.0 7.4 all-to-all-start.3
  200.4 8.1 copy.95
  208.5 7.8 copy.131
  218.2 8.2 convolution_convert_fusion.5
  227.8 4.4 copy.97
  232.1 65.2 %all-to-all-done.3 = bf16[32,2,64,512]{3,2,1,0:T(8,128)(2,1)} async-done(((bf16[32,2,64,512]{3,2,1,0:T(8,128)(2,1)}), bf16[32,2,64,512]{3,2,1,0:T(8,128)(2,1)}, u32[]{:S(2)}, u32[]{:S(2)}) %all-to-all-start.3) | async-done | bytes 4194336 | tf_op jit(solution)/shard_map/all_to_all | solution.py:134
  297.3 6.4 all-to-all-start.1
  303.8 96.6 %all-to-all-done.1 = bf16[32,2,64,512]{3,2,1,0:T(8,128)(2,1)} async-done(((bf16[32,2,64,512]{3,2,1,0:T(8,128)(2,1)}), bf16[32,2,64,512]{3,2,1,0:T(8,128)(2,1)}, u32[]{:S(2)}, u32[]{:S(2)}) %all-to-all-start.1) | async-done | bytes 4194336 | tf_op jit(solution)/shard_map/all_to_all | solution.py:133
  400.4 177.5 %while.19 = (s32[]{:T(128)}, f32[256,1,128]{0,2,1:T(8,128)S(1)}, f32[256,1,128]{0,2,1:T(8,128)S(1)}, bf16[8,8,64,512]{3,2,1,0:T(8,128)(2,1)}, bf16[8,8,64,128]{3...) while((s32[]{:T(128)}, f32[256,1,128]{0,2,1:T(8,128)S(1)}, ...), condition=%wide.region_9.10_spmd.clone, body=%wide.region_1.9_spmd.clone.sunk | while | flops 851605504 | bytes 56675696 | solution.py:178
  400.8 2.1 constant_dynamic-slice_fusion.3
  407.3 2.0 reshape.289
  417.8 2.1 fusion.133
  423.0 2.1 constant_dynamic-slice_fusion.3
  429.5 2.0 reshape.289
  440.0 2.1 fusion.133
  445.1 2.1 constant_dynamic-slice_fusion.3
  451.7 2.0 reshape.289
  462.1 2.1 fusion.133
  467.2 2.1 constant_dynamic-slice_fusion.3
  473.8 2.0 reshape.289
  484.2 2.1 fusion.133
  489.4 2.1 constant_dynamic-slice_fusion.3
  506.4 2.1 fusion.133
  511.5 2.1 constant_dynamic-slice_fusion.3
  528.5 2.1 fusion.133
  533.7 2.1 constant_dynamic-slice_fusion.3
  550.7 2.1 fusion.133
  555.8 2.1 constant_dynamic-slice_fusion.3
  572.8 2.1 fusion.133
  577.9 6.5 copy.104
  584.5 103.7 %all_to_all.41 = bf16[32,2,64,512]{3,1,2,0:T(2,128)(2,1)S(1)} all-to-all(bf16[32,2,64,512]{3,1,2,0:T(2,128)(2,1)S(1)} %copy.104), channel_id=1, replica_groups=mesh['dom'=32,'tp'=8] {'dom'}, dimensions={0} | all-to-all | bytes 8388608 | tf_op jit(solution)/shard_map/all_to_all | solution.py:180
  688.2 2.4 bitcast_convert_fusion
  691.1 9.2 %fusion.58 = bf16[4096,512]{0,1:T(8,128)(2,1)} fusion(bf16[896,512]{1,0:T(8,128)(2,1)S(1)} %bitcast.279, bf16[896,4096]{1,0:T(8,128)(2,1)} %bitcast.273), kind=kOutput, calls=%fused_computation.77 | convolution fusion | flops 3760193536 | bytes 12451840 | tf_op jit(solution)/shard_map/tc,tq->cq/dot_general | solution.py:210
  700.3 6.5 copy.129
  708.0 2.0 copy.107
  710.0 3.9 all-to-all-start.6
  714.0 2.1 copy.109
  716.1 27.9 %all-to-all-done.6 = bf16[32,2,64,128]{3,1,2,0:T(2,128)(2,1)S(1)} async-done(((bf16[32,2,64,128]{3,1,2,0:T(2,128)(2,1)}), bf16[32,2,64,128]{3,1,2,0:T(2,128)(2,1)S(1)}, u32[]{:S(2)}, u32[]{:S(2)}) %all-to-all-start.6) | async-done | bytes 1048608 | tf_op jit(solution)/shard_map/all_to_all | solution.py:187
  744.0 3.9 all-to-all-start.7
  750.9 29.1 %all-to-all-done.7 = bf16[32,2,64,128]{3,1,2,0:T(2,128)(2,1)S(1)} async-done(((bf16[32,2,64,128]{3,1,2,0:T(2,128)(2,1)}), bf16[32,2,64,128]{3,1,2,0:T(2,128)(2,1)S(1)}, u32[]{:S(2)}, u32[]{:S(2)}) %all-to-all-start.7) | async-done | bytes 1048608 | tf_op jit(solution)/shard_map/all_to_all | solution.py:194
  781.5 57.3 %reduce-scatter.4.cloned.1.call-done = bf16[128,512]{1,0:T(8,128)(2,1)} async-done(((bf16[4096,512]{1,0:T(8,128)(2,1)}), bf16[128,512]{1,0:T(8,128)(2,1)}) %reduce-scatter.4.cloned.1.call-update) | async-done | bytes 131088
  (349 shorter events, 151.6 us)
Async XLA Ops:
  7.2 16.4 %copy-start.12 = (bf16[14,64,128]{2,1,0:T(8,128)(2,1)S(1)}, bf16[14,64,128]{2,1,0:T(8,128)(2,1)}, u32[]{:S(2)}) copy-start(bf16[14,64,128]{2,1,0:T(8,128)(2,1)} %param.13) | copy-start | bytes 688132
  11.8 75.5 %copy-start.11 = (bf16[14,64,512]{2,1,0:T(8,128)(2,1)S(1)}, bf16[14,64,512]{2,1,0:T(8,128)(2,1)}, u32[]{:S(2)}) copy-start(bf16[14,64,512]{2,1,0:T(8,128)(2,1)} %param.11) | copy-start | bytes 2752516
  11.8 41.7 %all-to-all-start.4 = ((bf16[32,2,64,128]{3,2,1,0:T(8,128)(2,1)}), bf16[32,2,64,128]{3,2,1,0:T(8,128)(2,1)}, u32[]{:S(2)}, u32[]{:S(2)}) async-start(bf16[32,2,64,128]{3,2,1,0:T(8,128)(2,1)} %copy.103), calls=%async_computation.4 | async-start | bytes 2097152 | tf_op jit(solution)/shard_map/all_to_all | solution.py:136
  91.2 6.1 copy-start.10
  91.2 6.1 copy-start.13
  91.2 101.8 %all-to-all-start = ((bf16[8,14,64,512]{3,2,1,0:T(8,128)(2,1)}), bf16[8,14,64,512]{3,2,1,0:T(8,128)(2,1)}, u32[]{:S(2)}, u32[]{:S(2)}) async-start(bf16[8,14,64,512]{3,2,1,0:T(8,128)(2,1)} %stack.2), calls=%async_computation | async-start | bytes 14680064 | tf_op jit(solution)/shard_map/all_to_all | solution.py:90
  96.6 121.6 %all-gather.2.cloned.1.call-start = ((), (), s32[]{:S(2)}) async-start(), calls=%async_computation.9 | async-start | bytes 4325376 | tf_op jit(solution)/shard_map/all_gather | solution.py:103
  193.0 104.3 %all-to-all-start.3 = ((bf16[32,2,64,512]{3,2,1,0:T(8,128)(2,1)}), bf16[32,2,64,512]{3,2,1,0:T(8,128)(2,1)}, u32[]{:S(2)}, u32[]{:S(2)}) async-start(bf16[32,2,64,512]{3,2,1,0:T(8,128)(2,1)} %copy.101), calls=%async_computation.3 | async-start | bytes 8388608 | tf_op jit(solution)/shard_map/all_to_all | solution.py:134
  232.1 168.3 %copy-start.7 = (bf16[1,256,128]{2,1,0:T(8,128)(2,1)S(1)}, bf16[1,256,128]{2,1,0:T(8,128)(2,1)}, u32[]{:S(2)}) copy-start(bf16[1,256,128]{2,1,0:T(8,128)(2,1)} %param.15) | copy-start | bytes 196612
  297.3 103.1 %all-to-all-start.1 = ((bf16[32,2,64,512]{3,2,1,0:T(8,128)(2,1)}), bf16[32,2,64,512]{3,2,1,0:T(8,128)(2,1)}, u32[]{:S(2)}, u32[]{:S(2)}) async-start(bf16[32,2,64,512]{3,2,1,0:T(8,128)(2,1)} %copy.97), calls=%async_computation.1 | async-start | bytes 8388608 | tf_op jit(solution)/shard_map/all_to_all | solution.py:133
  303.7 535.1 %reduce-scatter.4.cloned.1.call-start = ((), (), s32[]{:S(2)}) async-start(), calls=%async_computation.10 | async-start | bytes 4325376
  412.5 2.2 copy-start.4
  414.3 3.5 copy-start.1
  414.3 5.5 copy-start.6
  417.8 4.7 copy-start.3
  434.7 2.2 copy-start.4
  436.5 2.0 copy-start.2
  436.5 3.5 copy-start.1
  436.5 5.5 copy-start.6
  440.0 4.7 copy-start.3
  456.9 2.2 copy-start.4
  458.7 3.4 copy-start.1
  458.7 5.5 copy-start.6
  462.1 4.7 copy-start.3
  479.0 2.2 copy-start.4
  480.8 3.4 copy-start.1
  480.8 5.5 copy-start.6
  484.2 4.7 copy-start.3
  501.1 2.2 copy-start.4
  502.9 3.5 copy-start.1
  502.9 5.5 copy-start.6
  506.4 4.7 copy-start.3
  523.3 2.2 copy-start.4
  525.1 2.0 copy-start.2
  525.1 3.4 copy-start.1
  525.1 5.5 copy-start.6
  528.5 4.7 copy-start.3
  545.4 2.2 copy-start.4
  547.2 3.4 copy-start.1
  547.2 5.5 copy-start.6
  550.7 4.7 copy-start.3
  567.5 2.2 copy-start.4
  569.3 3.4 copy-start.1
  569.3 5.5 copy-start.6
  572.8 4.7 copy-start.3
  706.8 7.2 copy-start.9
  710.0 33.9 %all-to-all-start.6 = ((bf16[32,2,64,128]{3,1,2,0:T(2,128)(2,1)}), bf16[32,2,64,128]{3,1,2,0:T(2,128)(2,1)S(1)}, u32[]{:S(2)}, u32[]{:S(2)}) async-start(bf16[32,2,64,128]{3,1,2,0:T(2,128)(2,1)} %copy.107), calls=%async_computation.6 | async-start | bytes 2097152 | tf_op jit(solution)/shard_map/all_to_all | solution.py:187
  744.0 36.0 %all-to-all-start.7 = ((bf16[32,2,64,128]{3,1,2,0:T(2,128)(2,1)}), bf16[32,2,64,128]{3,1,2,0:T(2,128)(2,1)S(1)}, u32[]{:S(2)}, u32[]{:S(2)}) async-start(bf16[32,2,64,128]{3,1,2,0:T(2,128)(2,1)} %copy.109), calls=%async_computation.7 | async-start | bytes 2097152 | tf_op jit(solution)/shard_map/all_to_all | solution.py:194
  (31 other events, 56.1 us)
Sparse Core Ops, SparseCore 0:
  100.2 117.9 all-gather.1
  706.9 131.8 reduce-scatter.3
